TPU v7x, 128 devices: a whole 4x4x4 slice. The times are simulated.
128 devices in a mesh: tok: 16 (over y, z), own: 8 (over x, core).
Axes of the slice: x: 4, y: 4, z: 4, core: 2. Of those that a mesh axis runs over, the one named last changes fastest.
Arguments:
- tokens: bfloat16 [16384, 1152], P(('tok', 'own')), may hold values from -6 to 6
- norm_gain: bfloat16 [1152], replicated, may hold values from 0.099609375 to 1.8984375
- w_query: bfloat16 [1152, 1152], replicated, as said below
- w_key: bfloat16 [1152, 384], replicated, as said below
- w_value: bfloat16 [1152, 384], replicated, may hold values from -0.1875 to 0.1875
- w_output: bfloat16 [1152, 1152], replicated, may hold values from -0.1875 to 0.1875
- qkv_in: bfloat16 [64, 48, 1152], P('own', None, 'tok'), may hold values from -0.1875 to 0.1875
- q_out: bfloat16 [64, 16, 1152], P('own', None, 'tok'), may hold values from -1.5 to 1.5
- kv_out: bfloat16 [64, 32, 384], P('own', None, 'tok'), may hold values from -1.5 to 1.5
- o_in: bfloat16 [64, 16, 1152], P('own', None, 'tok'), may hold values from -0.1875 to 0.1875
- o_out: bfloat16 [64, 16, 1152], P('own', None, 'tok'), may hold values from -1.5 to 1.5
- lengths: int32 [64], replicated, may hold values from 32 to 1536, as said below
- prompt_adapter: int32 [64], replicated, may hold values from 0 to 63
- adapter_slot: int32 [64], replicated, may hold values from 0 to 63, each once
Outputs:
- mixed: bfloat16 [16384, 1152], P(('tok', 'own'))
- kv_cache: bfloat16 [16384, 768], P(('tok', 'own'))
Inputs may be any that keep to these rules, and one draw needn't show every extreme that they name: `w_query`: entries lie within 6 / sqrt(1152) of zero. `w_key`: entries lie within 6 / sqrt(1152) of zero. `lengths`: lengths sum to 16384; exactly 8 prompts are 1536 long; the others hold 32 to 128 tokens, and one of them exactly 32. `adapter_slot`: each slot appears once; slot s is row s of the adapter tables, held by own index s // 8.
All inputs are finite; a program needn't handle non-finite values.
Results may differ from a plain program's by a relative error of at most 0.02.
Values may be sent and summed in bfloat16 or wider, within the bound.
No kernel may reach another device: no remote copies, remote signals or barrier semaphores. Data moves between devices by JAX's collectives and lax.ppermute only.
A program may use at most 128 MiB of HBM per device.

v0:
```python
import math
import jax
import jax.numpy as jnp
from jax import lax
from jax.sharding import PartitionSpec as P

D = 1152
HEADS = 18
KV_HEADS = 6
HEAD_WIDTH = 64
RANK = 16
REACH = 12
KVW = 384
SEG_DEV = 5
EPS = 1e-05
THETA = 10000.0


def from_behind(block, axis, distance):
    devices = range(lax.axis_size(axis))
    route = [(i - distance, i) for i in devices if i - distance in devices]
    return lax.ppermute(block, axis, route)


def rms_norm(row_block, gain_vec):
    widened = row_block.astype(jnp.float32)
    inverse_rms = lax.rsqrt(jnp.mean(widened * widened, axis=-1, keepdims=True) + EPS)
    return (widened * inverse_rms * gain_vec.astype(jnp.float32)).astype(jnp.bfloat16)


def prompt_index(positions, lengths):
    prompt_ends = jnp.cumsum(lengths)
    prompt_starts = prompt_ends - lengths
    inside = (positions[:, None] >= prompt_starts[None, :]).astype(jnp.int32)
    segment = jnp.sum(inside, axis=1) - 1
    members = jnp.arange(lengths.shape[0], dtype=jnp.int32)[None, :] == segment[:, None]
    offset = positions - jnp.sum(jnp.where(members, prompt_starts[None, :], 0), axis=1)
    return (segment, offset, members)


def slot_lookup(adapter, adapter_slot):
    matches = jnp.arange(adapter_slot.shape[0], dtype=jnp.int32)[None, :] == adapter[:, None]
    return jnp.sum(jnp.where(matches, adapter_slot[None, :], 0), axis=1)


def rotate(vectors, offset):
    half_dim = vectors.shape[-1] // 2
    frequency = jnp.exp(
        jnp.arange(half_dim, dtype=jnp.float32) * (-2.0 * math.log(THETA) / vectors.shape[-1])
    )
    angles = offset.astype(jnp.float32)[:, None] * frequency[None, :]
    cosine = jnp.cos(angles)[:, None, :]
    sine_table = jnp.sin(angles)[:, None, :]
    first_half = vectors[..., :half_dim]
    second_half = vectors[..., half_dim:]
    return jnp.concatenate(
        [
            first_half * cosine - second_half * sine_table,
            second_half * cosine + first_half * sine_table,
        ],
        axis=-1,
    )


def adapter_terms(row_block, code_rows, a_in, pieces):
    table_count, rank_cols, in_width = a_in.shape
    projected = lax.dot_general(
        row_block,
        a_in.reshape(table_count * rank_cols, in_width),
        (((1,), (1,)), ((), ())),
        preferred_element_type=jnp.float32,
    )
    chosen = (jnp.arange(table_count, dtype=jnp.int32)[None, :] == code_rows[:, None]).astype(
        jnp.float32
    )
    low_rank = (projected.reshape(-1, table_count, rank_cols) * chosen[:, :, None]).astype(
        jnp.bfloat16
    )
    results = []
    for col_start, b_table in pieces:
        width_rank = b_table.shape[1]
        section = low_rank[:, :, col_start : col_start + width_rank].reshape(
            -1, table_count * width_rank
        )
        results.append(
            jnp.dot(
                section,
                b_table.reshape(table_count * width_rank, b_table.shape[2]),
                preferred_element_type=jnp.float32,
            ).astype(jnp.bfloat16)
        )
    return tuple(results)


def on_device(
    tokens,
    norm_gain,
    w_query,
    w_key,
    w_value,
    w_output,
    qkv_in,
    q_out,
    kv_out,
    o_in,
    o_out,
    lengths,
    prompt_adapter,
    adapter_slot,
):
    tok_rows = tokens.shape[0]
    tok_count = lax.axis_size("tok")
    own_count = lax.axis_size("own")
    per_owner = qkv_in.shape[0]
    device_here = lax.axis_index(("tok", "own"))
    positions = device_here * tok_rows + jnp.arange(tok_rows, dtype=jnp.int32)
    segment, offset, members = prompt_index(positions, lengths)
    prompt_count = lengths.shape[0]
    first_segment = segment[0]
    code_rows = segment - first_segment
    normed = rms_norm(tokens, norm_gain)
    tables = (qkv_in, q_out, kv_out, o_in, o_out)
    table_shapes = tuple((table.shape[1:] for table in tables))
    packed = jnp.concatenate([table.reshape(per_owner, -1) for table in tables], axis=1)
    all_slots = lax.all_gather(packed, "own", axis=0, tiled=True)
    own_here = lax.axis_index("own")
    group_blocks = jnp.arange(tok_count, dtype=jnp.int32) * own_count + own_here
    prompt_starts = jnp.cumsum(lengths) - lengths
    group_first = (
        jnp.sum(
            (group_blocks[:, None] * tok_rows >= prompt_starts[None, :]).astype(jnp.int32), axis=1
        )
        - 1
    )
    group_segments = jnp.minimum(
        group_first[:, None] + jnp.arange(SEG_DEV, dtype=jnp.int32)[None, :], prompt_count - 1
    )
    group_slots = jnp.take(adapter_slot, jnp.take(prompt_adapter, group_segments))
    outgoing = jnp.take(all_slots, group_slots.reshape(-1), axis=0).reshape(
        tok_count, SEG_DEV, packed.shape[1]
    )
    incoming = lax.all_to_all(outgoing, "tok", 0, 0, tiled=True)
    selected = []
    col = 0
    for table_shape in table_shapes:
        width = table_shape[0] * table_shape[1]
        piece = incoming[:, :, col : col + width].reshape(
            tok_count, SEG_DEV, table_shape[0], table_shape[1]
        )
        col += width
        selected.append(
            jnp.transpose(piece, (1, 2, 0, 3)).reshape(
                SEG_DEV, table_shape[0], tok_count * table_shape[1]
            )
        )
    input_maps, query_maps, keyvalue_maps, output_in_maps, output_out_maps = selected
    delta_q, delta_k, delta_v = adapter_terms(
        normed,
        code_rows,
        input_maps,
        ((0, query_maps), (RANK, keyvalue_maps[:, :RANK]), (2 * RANK, keyvalue_maps[:, RANK:])),
    )
    base_q = jnp.dot(normed, w_query, preferred_element_type=jnp.float32)
    base_k = jnp.dot(normed, w_key, preferred_element_type=jnp.float32)
    base_v = jnp.dot(normed, w_value, preferred_element_type=jnp.float32)
    query_lin = (base_q + delta_q.astype(jnp.float32)).reshape(tok_rows, HEADS, HEAD_WIDTH)
    queries = rotate(query_lin, offset).reshape(tok_rows, D).astype(jnp.bfloat16)
    key_lin = (base_k + delta_k.astype(jnp.float32)).reshape(tok_rows, KV_HEADS, HEAD_WIDTH)
    key_rows = rotate(key_lin, offset).reshape(tok_rows, KVW).astype(jnp.bfloat16)
    value_rows = (base_v + delta_v.astype(jnp.float32)).astype(jnp.bfloat16)
    key_value = jnp.concatenate([key_rows, value_rows], axis=1)
    key_store = jnp.zeros(((REACH + 1) * tok_rows, 2 * KVW), jnp.bfloat16)
    key_store = lax.dynamic_update_slice_in_dim(key_store, key_value, REACH * tok_rows, 0)
    window = key_store
    moving = key_value
    for turn_index in range(REACH):
        moving = from_behind(moving, ("tok", "own"), 1)
        window = lax.dynamic_update_slice_in_dim(
            window, moving, (REACH - 1 - turn_index) * tok_rows, 0
        )
    key_positions = (
        device_here * tok_rows
        - REACH * tok_rows
        + jnp.arange((REACH + 1) * tok_rows, dtype=jnp.int32)
    )
    key_segment = prompt_index(key_positions, lengths)[0]
    allowed = (segment[:, None] == key_segment[None, :]) & (
        key_positions[None, :] <= positions[:, None]
    )
    groups = HEADS // KV_HEADS
    key_count = window.shape[0]
    query_head_rows = queries.reshape(tok_rows, KV_HEADS, groups, HEAD_WIDTH)
    key_head_rows = window[:, :KVW].reshape(key_count, KV_HEADS, HEAD_WIDTH)
    value_head_rows = window[:, KVW:].reshape(key_count, KV_HEADS, HEAD_WIDTH)
    score_matrix = jnp.einsum(
        "qkzr,ckr->kzqc", query_head_rows, key_head_rows, preferred_element_type=jnp.float32
    ) * HEAD_WIDTH ** (-0.5)
    score_matrix = jnp.where(allowed[None, None], score_matrix, -1e30)
    top_score = jnp.max(score_matrix, axis=-1, keepdims=True)
    exp_scores = jnp.exp(score_matrix - top_score)
    row_total = jnp.sum(exp_scores, axis=-1)
    rounded_values = exp_scores.astype(jnp.bfloat16)
    summed_rows = jnp.einsum(
        "iyxv,vip->xiyp", rounded_values, value_head_rows, preferred_element_type=jnp.float32
    )
    attn_rows = (
        (summed_rows / jnp.transpose(row_total, (2, 0, 1))[..., None])
        .reshape(tok_rows, D)
        .astype(jnp.bfloat16)
    )
    delta_o = adapter_terms(attn_rows, code_rows, output_in_maps, ((0, output_out_maps),))[0]
    projected_out = jnp.dot(
        attn_rows, w_output, preferred_element_type=jnp.float32
    ) + delta_o.astype(jnp.float32)
    mixed_rows = (tokens.astype(jnp.float32) + projected_out).astype(jnp.bfloat16)
    return (mixed_rows, key_value)


def solution(mesh):
    return jax.shard_map(
        on_device,
        mesh=mesh,
        in_specs=(
            P(("tok", "own"), None),
            P(),
            P(),
            P(),
            P(),
            P(),
            P("own", None, "tok"),
            P("own", None, "tok"),
            P("own", None, "tok"),
            P("own", None, "tok"),
            P("own", None, "tok"),
            P(),
            P(),
            P(),
        ),
        out_specs=(P(("tok", "own"), None), P(("tok", "own"), None)),
        check_vma=False,
    )
```

profile of v0, /device:TPU:24, one launch (start us, length us, event | category | flops | bytes accessed | tf_op | source)
XLA Modules:
  0.0 273.8 jit_solution(17576496565474559692)
XLA Ops:
  9.0 15.0 %all_gather.3 = bf16[64,7680]{1,0:T(8,128)(2,1)} all-gather(bf16[8,7680]{1,0:T(8,128)(2,1)S(1)} %constant_dynamic-update-slice_fusion), channel_id=1, replica_groups=mesh['tok'=16,'own'=8] {'own'}, dimensions={0}, use_global_device_ids=true | all-gather | bytes 1105920 | tf_op jit(solution)/shard_map/all_gather | solution.py:125
  24.0 4.8 %gather_fusion = bf16[80,7680]{1,0:T(8,128)(2,1)} fusion(bf16[64,7680]{1,0:T(8,128)(2,1)} %all_gather.3, s32[1024]{0:T(1024)S(1)} %pad_clamp_fusion), kind=kCustom, calls=%fused_computation.2 | custom fusion | bytes 2457920 | tf_op jit(solution)/shard_map/jit(_take)/gather | solution.py:139
  28.8 2.6 gather.10
  31.5 3.1 %broadcast_select_fusion = bf16[16,5,7680]{2,1,0:T(8,128)(2,1)} fusion(bf16[16,5,7680]{2,1,0:T(8,128)(2,1)} %gather.10, pred[16,5]{1,0:T(8,128)(4,1)S(1)} %get-tuple-element.3), kind=kLoop, calls=%fused_computation.18 | loop fusion | flops 614400 | bytes 2457680 | tf_op jit(solution)/shard_map/jit(_take)/select_n | solution.py:139
  34.6 8.3 %all-to-all-start = ((bf16[16,5,7680]{2,1,0:T(8,128)(2,1)}), bf16[16,5,7680]{2,1,0:T(8,128)(2,1)}, u32[]{:S(2)}, u32[]{:S(2)}) async-start(bf16[16,5,7680]{2,1,0:T(8,128)(2,1)} %broadcast_select_fusion), calls=%async_computation | async-start | bytes 3932160 | tf_op jit(solution)/shard_map/all_to_all | solution.py:142
  44.9 25.3 %all-to-all-done = bf16[16,5,7680]{2,1,0:T(8,128)(2,1)} async-done(((bf16[16,5,7680]{2,1,0:T(8,128)(2,1)}), bf16[16,5,7680]{2,1,0:T(8,128)(2,1)}, u32[]{:S(2)}, u32[]{:S(2)}) %all-to-all-start) | async-done | bytes 1228832 | tf_op jit(solution)/shard_map/all_to_all | solution.py:142
  73.0 2.2 copy.47
  75.2 2.3 reshape.335
  78.9 2.7 reshape.333
  81.5 2.4 copy.45
  84.0 2.2 dot_general.41
  95.0 9.3 %collective-permute-done = bf16[128,768]{1,0:T(8,128)(2,1)S(1)} collective-permute-done((bf16[128,768]{1,0:T(8,128)(2,1)S(1)}, bf16[128,768]{1,0:T(8,128)(2,1)S(1)}, u32[]{:S(2)}, u32[]{:S(2)}) %collective-permute-start) | collective-permute-done | bytes 196640 | tf_op jit(solution)/shard_map/ppermute | solution.py:22
  104.2 2.1 collective-permute-start.1
  107.4 8.1 %collective-permute-done.1 = bf16[128,768]{1,0:T(8,128)(2,1)} collective-permute-done((bf16[128,768]{1,0:T(8,128)(2,1)S(1)}, bf16[128,768]{1,0:T(8,128)(2,1)}, u32[]{:S(2)}, u32[]{:S(2)}) %collective-permute-start.1) | collective-permute-done | bytes 196640 | tf_op jit(solution)/shard_map/ppermute | solution.py:22
  117.5 2.0 fusion.43
  123.8 2.0 reshape_reshape.9
  139.9 8.5 %collective-permute-done.3 = bf16[128,768]{1,0:T(8,128)(2,1)S(1)} collective-permute-done((bf16[128,768]{1,0:T(8,128)(2,1)}, bf16[128,768]{1,0:T(8,128)(2,1)S(1)}, u32[]{:S(2)}, u32[]{:S(2)}) %collective-permute-start.3) | collective-permute-done | bytes 196640 | tf_op jit(solution)/shard_map/ppermute | solution.py:22
  150.3 2.2 convolution_add_fusion.1
  152.5 2.1 copy.54
  154.9 4.8 %collective-permute-done.4 = bf16[128,768]{1,0:T(8,128)(2,1)} collective-permute-done((bf16[128,768]{1,0:T(8,128)(2,1)S(1)}, bf16[128,768]{1,0:T(8,128)(2,1)}, u32[]{:S(2)}, u32[]{:S(2)}) %collective-permute-start.4) | collective-permute-done | bytes 196640 | tf_op jit(solution)/shard_map/ppermute | solution.py:22
  161.8 9.4 %collective-permute-done.5 = bf16[128,768]{1,0:T(8,128)(2,1)S(1)} collective-permute-done((bf16[128,768]{1,0:T(8,128)(2,1)}, bf16[128,768]{1,0:T(8,128)(2,1)S(1)}, u32[]{:S(2)}, u32[]{:S(2)}) %collective-permute-start.5) | collective-permute-done | bytes 196640 | tf_op jit(solution)/shard_map/ppermute | solution.py:22
  173.1 9.2 %collective-permute-done.6 = bf16[128,768]{1,0:T(8,128)(2,1)S(1)} collective-permute-done((bf16[128,768]{1,0:T(8,128)(2,1)S(1)}, bf16[128,768]{1,0:T(8,128)(2,1)S(1)}, u32[]{:S(2)}, u32[]{:S(2)}) %collective-permute-start.6) | collective-permute-done | bytes 196640 | tf_op jit(solution)/shard_map/ppermute | solution.py:22
  186.1 7.4 %collective-permute-done.7 = bf16[128,768]{1,0:T(8,128)(2,1)S(1)} collective-permute-done((bf16[128,768]{1,0:T(8,128)(2,1)S(1)}, bf16[128,768]{1,0:T(8,128)(2,1)S(1)}, u32[]{:S(2)}, u32[]{:S(2)}) %collective-permute-start.7) | collective-permute-done | bytes 196640 | tf_op jit(solution)/shard_map/ppermute | solution.py:22
  196.4 8.3 %collective-permute-done.8 = bf16[128,768]{1,0:T(8,128)(2,1)S(1)} collective-permute-done((bf16[128,768]{1,0:T(8,128)(2,1)S(1)}, bf16[128,768]{1,0:T(8,128)(2,1)S(1)}, u32[]{:S(2)}, u32[]{:S(2)}) %collective-permute-start.8) | collective-permute-done | bytes 196640 | tf_op jit(solution)/shard_map/ppermute | solution.py:22
  206.7 9.2 %collective-permute-done.9 = bf16[128,768]{1,0:T(8,128)(2,1)S(1)} collective-permute-done((bf16[128,768]{1,0:T(8,128)(2,1)S(1)}, bf16[128,768]{1,0:T(8,128)(2,1)S(1)}, u32[]{:S(2)}, u32[]{:S(2)}) %collective-permute-start.9) | collective-permute-done | bytes 196640 | tf_op jit(solution)/shard_map/ppermute | solution.py:22
  217.9 9.2 %collective-permute-done.10 = bf16[128,768]{1,0:T(8,128)(2,1)S(1)} collective-permute-done((bf16[128,768]{1,0:T(8,128)(2,1)S(1)}, bf16[128,768]{1,0:T(8,128)(2,1)S(1)}, u32[]{:S(2)}, u32[]{:S(2)}) %collective-permute-start.10) | collective-permute-done | bytes 196640 | tf_op jit(solution)/shard_map/ppermute | solution.py:22
  229.1 9.2 %collective-permute-done.11 = bf16[128,768]{1,0:T(8,128)(2,1)S(1)} collective-permute-done((bf16[128,768]{1,0:T(8,128)(2,1)S(1)}, bf16[128,768]{1,0:T(8,128)(2,1)S(1)}, u32[]{:S(2)}, u32[]{:S(2)}) %collective-permute-start.11) | collective-permute-done | bytes 196640 | tf_op jit(solution)/shard_map/ppermute | solution.py:22
  240.1 2.5 copy.51
  242.6 2.5 copy.50
  245.1 9.0 %fusion.2 = (f32[6,3,128]{2,1,0:T(4,128)S(1)}, f32[6,1664,128,3]{2,1,3,0:T(8,128)}) fusion(pred[128,1664]{0,1:T(8,128)(4,1)S(1)} %compare_and_fusion, bf16[1664,6,64,1]{0,2,3,1:T(8,128)(2,1)} %bitcast.101, bf16[128,6,3,64]{0,3,2,1:T(8,128)(2,1)S(1)} %bitcast.105), kind=kOutput, calls=%fused_computation.7 | convolution fusion | flops 502232832 | bytes 17130496 | tf_op jit(solution)/shard_map/qkzr,ckr->kzqc/dot_general | solution.py:195
  254.0 8.6 %fusion = f32[6,3,128]{2,1,0:T(4,128)S(1)} fusion(f32[6,1664,128,3]{2,1,3,0:T(8,128)} %get-tuple-element.17, f32[6,3,128]{2,1,0:T(4,128)S(1)} %get-tuple-element.16, pred[128,1664]{0,1:T(8,128)(4,1)S(1)} %compare_and_fusion), kind=kLoop, calls=%fused_computation.5 | loop fusion | flops 15333120 | bytes 15566848 | tf_op jit(solution)/shard_map/reduce_sum | solution.py:201
  262.7 9.2 %fusion.23 = bf16[128,6,3,64]{0,3,2,1:T(8,128)(2,1)S(1)} fusion(bf16[1664,6,64,1]{0,2,3,1:T(8,128)(2,1)S(1)} %bitcast.109, f32[6,1664,128,3]{2,1,3,0:T(8,128)} %get-tuple-element.17, f32[6,3,128]{2,1,0:T(4,128)S(1)} %get-tuple-element.16, pred[128,1664]{0,1:T(8,128)(4,1)S(1)} %compare_and_fusion, f32[128,6,3]{0,2,1:T(4,128)S(1)} %bitcast.116), kind=kOutput, calls=%fused_computation.34 | convolution fusion | flops 506363904 | bytes 17139712 | tf_op jit(solution)/shard_map/iyxv,vip->xiyp/dot_general | solution.py:203
  (173 shorter events, 66.3 us)
Async XLA Ops:
  0.6 149.7 %copy-start = (bf16[1152,1152]{1,0:T(8,128)(2,1)S(1)}, bf16[1152,1152]{1,0:T(8,128)(2,1)}, u32[]{:S(2)}) copy-start(bf16[1152,1152]{1,0:T(8,128)(2,1)} %param.18) | copy-start | bytes 7962628
  34.6 9.4 %copy-start.26 = (bf16[1152]{0:T(1024)(128)(2,1)S(1)}, bf16[1152]{0:T(1024)(128)(2,1)}, u32[]{:S(2)}) copy-start(bf16[1152]{0:T(1024)(128)(2,1)} %param.17) | copy-start | bytes 6916
  34.6 35.6 %all-to-all-start = ((bf16[16,5,7680]{2,1,0:T(8,128)(2,1)}), bf16[16,5,7680]{2,1,0:T(8,128)(2,1)}, u32[]{:S(2)}, u32[]{:S(2)}) async-start(bf16[16,5,7680]{2,1,0:T(8,128)(2,1)} %broadcast_select_fusion), calls=%async_computation | async-start | bytes 3932160 | tf_op jit(solution)/shard_map/all_to_all | solution.py:142
  42.9 27.3 %copy-start.29 = (s32[128]{0:T(128)}, s32[128]{0:T(128)S(1)}, u32[]{:S(2)}) copy-start(s32[128]{0:T(128)S(1)} %iota_add_fusion.1) | copy-start | bytes 1540
  43.2 27.0 %copy-start.31 = (s32[128]{0:T(128)}, s32[128]{0:T(128)S(1)}, u32[]{:S(2)}) copy-start(s32[128]{0:T(128)S(1)} %broadcast_add_fusion.1) | copy-start | bytes 1540
  44.0 42.1 %copy-start.18 = (f32[1152]{0:T(1024)}, f32[1152]{0:T(1024)S(1)}, u32[]{:S(2)}) copy-start(f32[1152]{0:T(1024)S(1)} %convert_element_type.91) | copy-start | bytes 13828
  44.1 42.1 %copy-start.25 = (f32[128]{0:T(128)}, f32[128]{0:T(128)S(1)}, u32[]{:S(2)}) copy-start(f32[128]{0:T(128)S(1)} %add_rsqrt_fusion) | copy-start | bytes 1540
  44.1 42.0 %copy-start.27 = (f32[128,5]{0,1:T(8,128)}, f32[128,5]{0,1:T(8,128)S(1)}, u32[]{:S(2)}) copy-start(f32[128,5]{0,1:T(8,128)S(1)} %fusion.34) | copy-start | bytes 7684
  44.9 45.6 %copy-start.15 = (f32[128,32]{0,1:T(8,128)}, f32[128,32]{0,1:T(8,128)S(1)}, u32[]{:S(2)}) copy-start(f32[128,32]{0,1:T(8,128)S(1)} %get-tuple-element.14) | copy-start | bytes 49156
  90.5 15.9 %copy-start.21 = (s32[1664]{0:T(1024)S(1)}, s32[1664]{0:T(1024)}, u32[]{:S(2)}) copy-start(s32[1664]{0:T(1024)} %copy-done.20) | copy-start | bytes 19972
  90.5 15.9 %copy-start.30 = (s32[128]{0:T(128)S(1)}, s32[128]{0:T(128)}, u32[]{:S(2)}) copy-start(s32[128]{0:T(128)} %copy-done.29) | copy-start | bytes 1540
  90.5 15.9 %copy-start.32 = (s32[128]{0:T(128)S(1)}, s32[128]{0:T(128)}, u32[]{:S(2)}) copy-start(s32[128]{0:T(128)} %copy-done.31) | copy-start | bytes 1540
  93.0 22.5 %copy-start.7 = (bf16[128,768]{1,0:T(8,128)(2,1)}, bf16[128,768]{1,0:T(8,128)(2,1)S(1)}, u32[]{:S(2)}) copy-start(bf16[128,768]{1,0:T(8,128)(2,1)S(1)} %pad_maximum_fusion.1) | copy-start | bytes 589828
  93.0 11.2 %collective-permute-start = (bf16[128,768]{1,0:T(8,128)(2,1)S(1)}, bf16[128,768]{1,0:T(8,128)(2,1)S(1)}, u32[]{:S(2)}, u32[]{:S(2)}) collective-permute-start(bf16[128,768]{1,0:T(8,128)(2,1)S(1)} %pad_maximum_fusion.1), channel_id=1, source_target_pairs={{0,1},{1,2},{2,3},{3,4},{4,5},{5,6},{6,7},{7,8},{8,9},{9,10},{10,1... | collective-permute-start | bytes 589832 | tf_op jit(solution)/shard_map/ppermute | solution.py:22
  104.2 11.3 %copy-start.10 = (bf16[128,768]{1,0:T(8,128)(2,1)}, bf16[128,768]{1,0:T(8,128)(2,1)S(1)}, u32[]{:S(2)}) copy-start(bf16[128,768]{1,0:T(8,128)(2,1)S(1)} %collective-permute-done) | copy-start | bytes 589828
  104.2 11.3 %collective-permute-start.1 = (bf16[128,768]{1,0:T(8,128)(2,1)S(1)}, bf16[128,768]{1,0:T(8,128)(2,1)}, u32[]{:S(2)}, u32[]{:S(2)}) collective-permute-start(bf16[128,768]{1,0:T(8,128)(2,1)S(1)} %collective-permute-done), channel_id=1, source_target_pairs={{0,1},{1,2},{2,3},{3,4},{4,5},{5,6},{6,7},{7,8},{8,9},{9,10},{10,1... | collective-permute-start | bytes 589832 | tf_op jit(solution)/shard_map/ppermute | solution.py:22
  115.5 21.4 %collective-permute-start.2 = (bf16[128,768]{1,0:T(8,128)(2,1)}, bf16[128,768]{1,0:T(8,128)(2,1)}, u32[]{:S(2)}, u32[]{:S(2)}) collective-permute-start(bf16[128,768]{1,0:T(8,128)(2,1)} %collective-permute-done.1), channel_id=1, source_target_pairs={{0,1},{1,2},{2,3},{3,4},{4,5},{5,6},{6,7},{7,8},{8,9},{9,10},{10,1... | collective-permute-start | bytes 589832 | tf_op jit(solution)/shard_map/ppermute | solution.py:22
  137.0 11.4 %collective-permute-start.3 = (bf16[128,768]{1,0:T(8,128)(2,1)}, bf16[128,768]{1,0:T(8,128)(2,1)S(1)}, u32[]{:S(2)}, u32[]{:S(2)}) collective-permute-start(bf16[128,768]{1,0:T(8,128)(2,1)} %collective-permute-done.2), channel_id=1, source_target_pairs={{0,1},{1,2},{2,3},{3,4},{4,5},{5,6},{6,7},{7,8},{8,9},{9,10},{10,1... | collective-permute-start | bytes 589832 | tf_op jit(solution)/shard_map/ppermute | solution.py:22
  139.9 14.8 %copy-start.8 = (bf16[128,768]{1,0:T(8,128)(2,1)S(1)}, bf16[128,768]{1,0:T(8,128)(2,1)}, u32[]{:S(2)}) copy-start(bf16[128,768]{1,0:T(8,128)(2,1)} %copy-done.7) | copy-start | bytes 589828
  148.4 11.3 %collective-permute-start.4 = (bf16[128,768]{1,0:T(8,128)(2,1)S(1)}, bf16[128,768]{1,0:T(8,128)(2,1)}, u32[]{:S(2)}, u32[]{:S(2)}) collective-permute-start(bf16[128,768]{1,0:T(8,128)(2,1)S(1)} %collective-permute-done.3), channel_id=1, source_target_pairs={{0,1},{1,2},{2,3},{3,4},{4,5},{5,6},{6,7},{7,8},{8,9},{9,10},{10,1... | collective-permute-start | bytes 589832 | tf_op jit(solution)/shard_map/ppermute | solution.py:22
  154.7 18.4 %copy-start.11 = (bf16[128,768]{1,0:T(8,128)(2,1)S(1)}, bf16[128,768]{1,0:T(8,128)(2,1)}, u32[]{:S(2)}) copy-start(bf16[128,768]{1,0:T(8,128)(2,1)} %copy-done.10) | copy-start | bytes 589828
  154.9 40.6 %copy-start.13 = (bf16[128,768]{1,0:T(8,128)(2,1)S(1)}, bf16[128,768]{1,0:T(8,128)(2,1)}, u32[]{:S(2)}) copy-start(bf16[128,768]{1,0:T(8,128)(2,1)} %copy-done.12) | copy-start | bytes 589828
  159.7 11.4 %collective-permute-start.5 = (bf16[128,768]{1,0:T(8,128)(2,1)}, bf16[128,768]{1,0:T(8,128)(2,1)S(1)}, u32[]{:S(2)}, u32[]{:S(2)}) collective-permute-start(bf16[128,768]{1,0:T(8,128)(2,1)} %collective-permute-done.4), channel_id=1, source_target_pairs={{0,1},{1,2},{2,3},{3,4},{4,5},{5,6},{6,7},{7,8},{8,9},{9,10},{10,1... | collective-permute-start | bytes 589832 | tf_op jit(solution)/shard_map/ppermute | solution.py:22
  171.1 11.2 %collective-permute-start.6 = (bf16[128,768]{1,0:T(8,128)(2,1)S(1)}, bf16[128,768]{1,0:T(8,128)(2,1)S(1)}, u32[]{:S(2)}, u32[]{:S(2)}) collective-permute-start(bf16[128,768]{1,0:T(8,128)(2,1)S(1)} %collective-permute-done.5), channel_id=1, source_target_pairs={{0,1},{1,2},{2,3},{3,4},{4,5},{5,6},{6,7},{7,8},{8,9},{9,10},{10,1... | collective-permute-start | bytes 589832 | tf_op jit(solution)/shard_map/ppermute | solution.py:22
  182.3 11.2 %collective-permute-start.7 = (bf16[128,768]{1,0:T(8,128)(2,1)S(1)}, bf16[128,768]{1,0:T(8,128)(2,1)S(1)}, u32[]{:S(2)}, u32[]{:S(2)}) collective-permute-start(bf16[128,768]{1,0:T(8,128)(2,1)S(1)} %collective-permute-done.6), channel_id=1, source_target_pairs={{0,1},{1,2},{2,3},{3,4},{4,5},{5,6},{6,7},{7,8},{8,9},{9,10},{10,1... | collective-permute-start | bytes 589832 | tf_op jit(solution)/shard_map/ppermute | solution.py:22
  193.5 11.2 %collective-permute-start.8 = (bf16[128,768]{1,0:T(8,128)(2,1)S(1)}, bf16[128,768]{1,0:T(8,128)(2,1)S(1)}, u32[]{:S(2)}, u32[]{:S(2)}) collective-permute-start(bf16[128,768]{1,0:T(8,128)(2,1)S(1)} %collective-permute-done.7), channel_id=1, source_target_pairs={{0,1},{1,2},{2,3},{3,4},{4,5},{5,6},{6,7},{7,8},{8,9},{9,10},{10,1... | collective-permute-start | bytes 589832 | tf_op jit(solution)/shard_map/ppermute | solution.py:22
  204.7 11.2 %collective-permute-start.9 = (bf16[128,768]{1,0:T(8,128)(2,1)S(1)}, bf16[128,768]{1,0:T(8,128)(2,1)S(1)}, u32[]{:S(2)}, u32[]{:S(2)}) collective-permute-start(bf16[128,768]{1,0:T(8,128)(2,1)S(1)} %collective-permute-done.8), channel_id=1, source_target_pairs={{0,1},{1,2},{2,3},{3,4},{4,5},{5,6},{6,7},{7,8},{8,9},{9,10},{10,1... | collective-permute-start | bytes 589832 | tf_op jit(solution)/shard_map/ppermute | solution.py:22
  215.9 11.2 %collective-permute-start.10 = (bf16[128,768]{1,0:T(8,128)(2,1)S(1)}, bf16[128,768]{1,0:T(8,128)(2,1)S(1)}, u32[]{:S(2)}, u32[]{:S(2)}) collective-permute-start(bf16[128,768]{1,0:T(8,128)(2,1)S(1)} %collective-permute-done.9), channel_id=1, source_target_pairs={{0,1},{1,2},{2,3},{3,4},{4,5},{5,6},{6,7},{7,8},{8,9},{9,10},{10,1... | collective-permute-start | bytes 589832 | tf_op jit(solution)/shard_map/ppermute | solution.py:22
  227.1 11.2 %collective-permute-start.11 = (bf16[128,768]{1,0:T(8,128)(2,1)S(1)}, bf16[128,768]{1,0:T(8,128)(2,1)S(1)}, u32[]{:S(2)}, u32[]{:S(2)}) collective-permute-start(bf16[128,768]{1,0:T(8,128)(2,1)S(1)} %collective-permute-done.10), channel_id=1, source_target_pairs={{0,1},{1,2},{2,3},{3,4},{4,5},{5,6},{6,7},{7,8},{8,9},{9,10},{10,1... | collective-permute-start | bytes 589832 | tf_op jit(solution)/shard_map/ppermute | solution.py:22
  262.7 9.3 %copy-start.14 = (bf16[5,16,1152]{2,1,0:T(8,128)(2,1)S(1)}, bf16[5,16,1152]{2,1,0:T(8,128)(2,1)}, u32[]{:S(2)}) copy-start(bf16[5,16,1152]{2,1,0:T(8,128)(2,1)} %dot_general.51) | copy-start | bytes 552964
  262.7 9.5 %copy-start.9 = (bf16[80,1152]{1,0:T(8,128)(2,1)S(1)}, bf16[80,1152]{1,0:T(8,128)(2,1)}, u32[]{:S(2)}) copy-start(bf16[80,1152]{1,0:T(8,128)(2,1)} %reshape_reshape.9) | copy-start | bytes 552964
  262.7 9.7 %copy-start.4 = (bf16[1152,1152]{1,0:T(8,128)(2,1)S(1)}, bf16[1152,1152]{1,0:T(8,128)(2,1)}, u32[]{:S(2)}) copy-start(bf16[1152,1152]{1,0:T(8,128)(2,1)} %param.21) | copy-start | bytes 7962628
  (14 other events, 70.6 us)
where the time goes:
time: 276 us; the launch traced here: 274 us
  waiting for transfers between devices  118 us (43%)
  local copies, waits for them, and re-layouts  62.1 us (22%)
  starting transfers between devices  31.4 us (11%)
  matrix products  28.8 us (10%)
  other arithmetic  16.9 us (6%)
  blocking collectives  15 us (5%)
    ppermute x12, waiting for transfers between devices, from_behind(): return lax.ppermute(block, axis, route)  92.7 us
    all_to_all x1, waiting for transfers between devices, on_device(): incoming = lax.all_to_all(outgoing, 'tok', 0, 0, tiled=True)  25.3 us
    ppermute x12, starting transfers between devices, from_behind(): return lax.ppermute(block, axis, route)  23.1 us
    all_gather x1, blocking collectives, on_device(): all_slots = lax.all_gather(packed, 'own', axis=0, tiled=True)  15 us
    dot_general x1, matrix products, on_device(): jnp.einsum('iyxv,vip->xiyp', rounded_values, value_head_rows, preferred_e...  9.21 us
    reshape x5, local copies, waits for them, and re-layouts, on_device(): incoming[:, :, col:col + width]  9 us
    dot_general x1, matrix products, on_device(): jnp.einsum('qkzr,ckr->kzqc', query_head_rows, key_head_rows, preferred_el...  8.99 us
    reduce_sum x1, other arithmetic, on_device(): row_total = jnp.sum(exp_scores, axis=-1)  8.61 us
  transfers between devices with their start and end apart: 13, of which 12 were waited for; matrix products, arithmetic and copies ran while one was open for 11% of the time, Pallas kernels for 0%

commit v1 on v0

--- a/solution.py
+++ b/solution.py
@@ -122,7 +122,23 @@
     tables = (qkv_in, q_out, kv_out, o_in, o_out)
     table_shapes = tuple((table.shape[1:] for table in tables))
     packed = jnp.concatenate([table.reshape(per_owner, -1) for table in tables], axis=1)
-    all_slots = lax.all_gather(packed, "own", axis=0, tiled=True)
+    size, index, rows = (lax.axis_size("own"), lax.axis_index("own"), packed.shape[0])
+    right = [(i_2, (i_2 + 1) % size) for i_2 in range(size)]
+    behind = [(i_2, (i_2 - 1) % size) for i_2 in range(size)]
+    all_slots = jnp.zeros((*packed.shape[:0], size * rows, *packed.shape[0 + 1 :]), packed.dtype)
+    all_slots = lax.dynamic_update_slice_in_dim(all_slots, packed, index * rows, axis=0)
+    from_left = from_right = packed
+    middle = size // 2
+    for step in range(1, middle + 1):
+        from_left = lax.ppermute(from_left, "own", right)
+        all_slots = lax.dynamic_update_slice_in_dim(
+            all_slots, from_left, (index - step) % size * rows, axis=0
+        )
+        if step < size - middle:
+            from_right = lax.ppermute(from_right, "own", behind)
+            all_slots = lax.dynamic_update_slice_in_dim(
+                all_slots, from_right, (index + step) % size * rows, axis=0
+            )
     own_here = lax.axis_index("own")
     group_blocks = jnp.arange(tok_count, dtype=jnp.int32) * own_count + own_here
     prompt_starts = jnp.cumsum(lengths) - lengths

time: 276 us -> 286 us (1.036)
  local copies, waits for them, and re-layouts: 62.1 us -> 80.5 us
  blocking collectives: 15 us -> 0 us
  starting transfers between devices: 31.4 us -> 39.8 us
  waiting for transfers between devices: 118 us -> 115 us
    all_gather x1 -> x0, blocking collectives: 15 us -> none  [on_device(): all_slots = lax.all_gather(packed, 'own', axis=0, tiled=True)]
    ppermute x0 -> x7, waiting for transfers between devices: none -> 9.54 us  [the longest x4 8.4 us: on_device(): from_left = lax.ppermute(from_left, 'own', right)]
    dynamic_update_slice x12, local copies, waits for them, and re-layouts: 2.96 us -> 12 us  [on_device(): lax.dynamic_update_slice_in_dim(window, moving, (REACH - 1 - turn_index)...]
    ppermute x0 -> x7, starting transfers between devices: none -> 8.23 us  [the longest x3 8.22 us: on_device(): from_right = lax.ppermute(from_right, 'own', behind)]
    ppermute x12, waiting for transfers between devices: 92.7 us -> 84.5 us  [from_behind(): return lax.ppermute(block, axis, route)]
    dynamic_update_slice x0 -> x8, local copies, waits for them, and re-layouts: none -> 5.25 us  [the longest x4 2.62 us: on_device(): lax.dynamic_update_slice_in_dim(all_slots, from_left, (index - step) % si...]
    all_to_all x1, waiting for transfers between devices: 25.3 us -> 21.2 us  [on_device(): incoming = lax.all_to_all(outgoing, 'tok', 0, 0, tiled=True)]
  transfers between devices with their start and end apart: 13 -> 20, of which waited for: 12 -> 15; matrix products, arithmetic and copies ran while one was open for 11% -> 19% of each run, Pallas kernels for 0% -> 0%
where the time goes in v1:
time: 286 us; the launch traced here: 284 us
  waiting for transfers between devices  115 us (40%)
  local copies, waits for them, and re-layouts  80.5 us (28%)
  starting transfers between devices  39.8 us (14%)
  matrix products  28.1 us (10%)
  other arithmetic  18.9 us (7%)
    ppermute x12, waiting for transfers between devices, from_behind(): return lax.ppermute(block, axis, route)  84.5 us
    ppermute x12, starting transfers between devices, from_behind(): return lax.ppermute(block, axis, route)  23.2 us
    all_to_all x1, waiting for transfers between devices, on_device(): incoming = lax.all_to_all(outgoing, 'tok', 0, 0, tiled=True)  21.2 us
    dynamic_update_slice x12, local copies, waits for them, and re-layouts, on_device(): lax.dynamic_update_slice_in_dim(window, moving, (REACH - 1 - turn_index)...  12 us
    dot_general x1, matrix products, on_device(): jnp.einsum('iyxv,vip->xiyp', rounded_values, value_head_rows, preferred_e...  9.21 us
    dot_general x1, matrix products, on_device(): jnp.einsum('qkzr,ckr->kzqc', query_head_rows, key_head_rows, preferred_el...  8.99 us
    reduce_sum x1, other arithmetic, on_device(): row_total = jnp.sum(exp_scores, axis=-1)  8.61 us
    ppermute x4, waiting for transfers between devices, on_device(): from_left = lax.ppermute(from_left, 'own', right)  8.4 us
  transfers between devices with their start and end apart: 20, of which 15 were waited for; matrix products, arithmetic and copies ran while one was open for 19% of the time, Pallas kernels for 0%

profile of v1, /device:TPU:24, one launch (start us, length us, event | category | flops | bytes accessed | tf_op | source)
XLA Modules:
  0.0 283.9 jit_solution(1797261672248460899)
XLA Ops:
  5.6 2.2 collective-permute-start.1
  16.6 2.9 %collective-permute-start.3 = (bf16[8,7680]{1,0:T(8,128)(2,1)S(1)}, bf16[8,7680]{1,0:T(8,128)(2,1)S(1)}, u32[]{:S(2)}, u32[]{:S(2)}) collective-permute-start(bf16[8,7680]{1,0:T(8,128)(2,1)S(1)} %collective-permute-done.1), channel_id=1, source_target_pairs={{0,7},{1,0},{2,1},{3,2},{4,3},{5,4},{6,5},{7,6},{8,15},{9,8},{10,9... | collective-permute-start | bytes 368648 | tf_op jit(solution)/shard_map/ppermute | solution.py:138
  22.0 3.1 %collective-permute-start.5 = (bf16[8,7680]{1,0:T(8,128)(2,1)S(1)}, bf16[8,7680]{1,0:T(8,128)(2,1)S(1)}, u32[]{:S(2)}, u32[]{:S(2)}) collective-permute-start(bf16[8,7680]{1,0:T(8,128)(2,1)S(1)} %collective-permute-done.3), channel_id=1, source_target_pairs={{0,7},{1,0},{2,1},{3,2},{4,3},{5,4},{6,5},{7,6},{8,15},{9,8},{10,9... | collective-permute-start | bytes 368648 | tf_op jit(solution)/shard_map/ppermute | solution.py:138
  26.3 4.2 %collective-permute-done.4 = bf16[8,7680]{1,0:T(8,128)(2,1)S(1)} collective-permute-done((bf16[8,7680]{1,0:T(8,128)(2,1)S(1)}, bf16[8,7680]{1,0:T(8,128)(2,1)S(1)}, u32[]{:S(2)}, u32[]{:S(2)}) %collective-permute-start.4) | collective-permute-done | bytes 122912 | tf_op jit(solution)/shard_map/ppermute | solution.py:133
  31.9 4.2 %collective-permute-done.6 = bf16[8,7680]{1,0:T(8,128)(2,1)S(1)} collective-permute-done((bf16[8,7680]{1,0:T(8,128)(2,1)S(1)}, bf16[8,7680]{1,0:T(8,128)(2,1)S(1)}, u32[]{:S(2)}, u32[]{:S(2)}) %collective-permute-start.6) | collective-permute-done | bytes 122912 | tf_op jit(solution)/shard_map/ppermute | solution.py:133
  36.7 4.8 %gather_fusion = bf16[80,7680]{1,0:T(8,128)(2,1)} fusion(bf16[64,7680]{1,0:T(8,128)(2,1)} %constant_dynamic-update-slice_fusion.17, s32[1024]{0:T(1024)S(1)} %pad_clamp_fusion), kind=kCustom, calls=%fused_computation.2 | custom fusion | bytes 2457920 | tf_op jit(solution)/shard_map/jit(_take)/gather | solution.py:155
  41.5 2.6 gather.10
  44.2 3.1 %broadcast_select_fusion = bf16[16,5,7680]{2,1,0:T(8,128)(2,1)} fusion(bf16[16,5,7680]{2,1,0:T(8,128)(2,1)} %gather.10, pred[16,5]{1,0:T(8,128)(4,1)S(1)} %get-tuple-element.3), kind=kLoop, calls=%fused_computation.18 | loop fusion | flops 614400 | bytes 2457680 | tf_op jit(solution)/shard_map/jit(_take)/select_n | solution.py:155
  47.3 8.3 %all-to-all-start = ((bf16[16,5,7680]{2,1,0:T(8,128)(2,1)}), bf16[16,5,7680]{2,1,0:T(8,128)(2,1)}, u32[]{:S(2)}, u32[]{:S(2)}) async-start(bf16[16,5,7680]{2,1,0:T(8,128)(2,1)} %broadcast_select_fusion), calls=%async_computation | async-start | bytes 3932160 | tf_op jit(solution)/shard_map/all_to_all | solution.py:158
  56.5 21.2 %all-to-all-done = bf16[16,5,7680]{2,1,0:T(8,128)(2,1)} async-done(((bf16[16,5,7680]{2,1,0:T(8,128)(2,1)}), bf16[16,5,7680]{2,1,0:T(8,128)(2,1)}, u32[]{:S(2)}, u32[]{:S(2)}) %all-to-all-start) | async-done | bytes 1228832 | tf_op jit(solution)/shard_map/all_to_all | solution.py:158
  80.8 2.3 reshape.335
  84.5 2.7 reshape.333
  87.1 2.4 copy.45
  89.6 2.2 dot_general.41
  100.6 9.3 %collective-permute-done.7 = bf16[128,768]{1,0:T(8,128)(2,1)S(1)} collective-permute-done((bf16[128,768]{1,0:T(8,128)(2,1)S(1)}, bf16[128,768]{1,0:T(8,128)(2,1)S(1)}, u32[]{:S(2)}, u32[]{:S(2)}) %collective-permute-start.7) | collective-permute-done | bytes 196640 | tf_op jit(solution)/shard_map/ppermute | solution.py:22
  112.8 8.3 %collective-permute-done.8 = bf16[128,768]{1,0:T(8,128)(2,1)} collective-permute-done((bf16[128,768]{1,0:T(8,128)(2,1)S(1)}, bf16[128,768]{1,0:T(8,128)(2,1)}, u32[]{:S(2)}, u32[]{:S(2)}) %collective-permute-start.8) | collective-permute-done | bytes 196640 | tf_op jit(solution)/shard_map/ppermute | solution.py:22
  147.5 8.5 %collective-permute-done.10 = bf16[128,768]{1,0:T(8,128)(2,1)S(1)} collective-permute-done((bf16[128,768]{1,0:T(8,128)(2,1)}, bf16[128,768]{1,0:T(8,128)(2,1)S(1)}, u32[]{:S(2)}, u32[]{:S(2)}) %collective-permute-start.10) | collective-permute-done | bytes 196640 | tf_op jit(solution)/shard_map/ppermute | solution.py:22
  159.4 2.1 copy.54
  161.5 5.8 %collective-permute-done.11 = bf16[128,768]{1,0:T(8,128)(2,1)} collective-permute-done((bf16[128,768]{1,0:T(8,128)(2,1)S(1)}, bf16[128,768]{1,0:T(8,128)(2,1)}, u32[]{:S(2)}, u32[]{:S(2)}) %collective-permute-start.11) | collective-permute-done | bytes 196640 | tf_op jit(solution)/shard_map/ppermute | solution.py:22
  170.5 8.3 %collective-permute-done.12 = bf16[128,768]{1,0:T(8,128)(2,1)S(1)} collective-permute-done((bf16[128,768]{1,0:T(8,128)(2,1)}, bf16[128,768]{1,0:T(8,128)(2,1)S(1)}, u32[]{:S(2)}, u32[]{:S(2)}) %collective-permute-start.12) | collective-permute-done | bytes 196640 | tf_op jit(solution)/shard_map/ppermute | solution.py:22
  182.4 7.6 %collective-permute-done.13 = bf16[128,768]{1,0:T(8,128)(2,1)S(1)} collective-permute-done((bf16[128,768]{1,0:T(8,128)(2,1)S(1)}, bf16[128,768]{1,0:T(8,128)(2,1)S(1)}, u32[]{:S(2)}, u32[]{:S(2)}) %collective-permute-start.13) | collective-permute-done | bytes 196640 | tf_op jit(solution)/shard_map/ppermute | solution.py:22
  195.1 6.1 %collective-permute-done.14 = bf16[128,768]{1,0:T(8,128)(2,1)S(1)} collective-permute-done((bf16[128,768]{1,0:T(8,128)(2,1)S(1)}, bf16[128,768]{1,0:T(8,128)(2,1)S(1)}, u32[]{:S(2)}, u32[]{:S(2)}) %collective-permute-start.14) | collective-permute-done | bytes 196640 | tf_op jit(solution)/shard_map/ppermute | solution.py:22
  205.5 6.9 %collective-permute-done.15 = bf16[128,768]{1,0:T(8,128)(2,1)S(1)} collective-permute-done((bf16[128,768]{1,0:T(8,128)(2,1)S(1)}, bf16[128,768]{1,0:T(8,128)(2,1)S(1)}, u32[]{:S(2)}, u32[]{:S(2)}) %collective-permute-start.15) | collective-permute-done | bytes 196640 | tf_op jit(solution)/shard_map/ppermute | solution.py:22
  215.7 7.9 %collective-permute-done.16 = bf16[128,768]{1,0:T(8,128)(2,1)S(1)} collective-permute-done((bf16[128,768]{1,0:T(8,128)(2,1)S(1)}, bf16[128,768]{1,0:T(8,128)(2,1)S(1)}, u32[]{:S(2)}, u32[]{:S(2)}) %collective-permute-start.16) | collective-permute-done | bytes 196640 | tf_op jit(solution)/shard_map/ppermute | solution.py:22
  226.9 7.9 %collective-permute-done.17 = bf16[128,768]{1,0:T(8,128)(2,1)S(1)} collective-permute-done((bf16[128,768]{1,0:T(8,128)(2,1)S(1)}, bf16[128,768]{1,0:T(8,128)(2,1)S(1)}, u32[]{:S(2)}, u32[]{:S(2)}) %collective-permute-start.17) | collective-permute-done | bytes 196640 | tf_op jit(solution)/shard_map/ppermute | solution.py:22
  238.1 7.9 %collective-permute-done.18 = bf16[128,768]{1,0:T(8,128)(2,1)S(1)} collective-permute-done((bf16[128,768]{1,0:T(8,128)(2,1)S(1)}, bf16[128,768]{1,0:T(8,128)(2,1)S(1)}, u32[]{:S(2)}, u32[]{:S(2)}) %collective-permute-start.18) | collective-permute-done | bytes 196640 | tf_op jit(solution)/shard_map/ppermute | solution.py:22
  246.7 3.5 %fusion.42 = (bf16[1664,384]{1,0:T(8,128)(2,1)}, bf16[1664,384]{1,0:T(8,128)(2,1)}) fusion(bf16[1664,768]{1,0:T(8,128)(2,1)} %constant_dynamic-update-slice_fusion.5), kind=kLoop, calls=%fused_computation.109 | loop fusion | bytes 5111808 | tf_op jit(solution)/shard_map/slice | solution.py:209
  250.1 2.5 copy.51
  252.7 2.5 copy.50
  255.2 9.0 %fusion.2 = (f32[6,3,128]{2,1,0:T(4,128)S(1)}, f32[6,1664,128,3]{2,1,3,0:T(8,128)}) fusion(pred[128,1664]{0,1:T(8,128)(4,1)S(1)} %compare_and_fusion, bf16[1664,6,64,1]{0,2,3,1:T(8,128)(2,1)} %bitcast.101, bf16[128,6,3,64]{0,3,2,1:T(8,128)(2,1)S(1)} %bitcast.105), kind=kOutput, calls=%fused_computation.7 | convolution fusion | flops 502232832 | bytes 17130496 | tf_op jit(solution)/shard_map/qkzr,ckr->kzqc/dot_general | solution.py:211
  264.2 8.6 %fusion = f32[6,3,128]{2,1,0:T(4,128)S(1)} fusion(f32[6,1664,128,3]{2,1,3,0:T(8,128)} %get-tuple-element.17, f32[6,3,128]{2,1,0:T(4,128)S(1)} %get-tuple-element.16, pred[128,1664]{0,1:T(8,128)(4,1)S(1)} %compare_and_fusion), kind=kLoop, calls=%fused_computation.5 | loop fusion | flops 15333120 | bytes 15566848 | tf_op jit(solution)/shard_map/reduce_sum | solution.py:217
  272.8 9.2 %fusion.23 = bf16[128,6,3,64]{0,3,2,1:T(8,128)(2,1)S(1)} fusion(bf16[1664,6,64,1]{0,2,3,1:T(8,128)(2,1)S(1)} %bitcast.109, f32[6,1664,128,3]{2,1,3,0:T(8,128)} %get-tuple-element.17, f32[6,3,128]{2,1,0:T(4,128)S(1)} %get-tuple-element.16, pred[128,1664]{0,1:T(8,128)(4,1)S(1)} %compare_and_fusion, f32[128,6,3]{0,2,1:T(4,128)S(1)} %bitcast.116), kind=kOutput, calls=%fused_computation.34 | convolution fusion | flops 506363904 | bytes 17139712 | tf_op jit(solution)/shard_map/iyxv,vip->xiyp/dot_general | solution.py:219
  (189 shorter events, 94.2 us)
Async XLA Ops:
  0.6 157.3 %copy-start = (bf16[1152,1152]{1,0:T(8,128)(2,1)S(1)}, bf16[1152,1152]{1,0:T(8,128)(2,1)}, u32[]{:S(2)}) copy-start(bf16[1152,1152]{1,0:T(8,128)(2,1)} %param.18) | copy-start | bytes 7962628
  5.6 11.0 %collective-permute-start.1 = (bf16[8,7680]{1,0:T(8,128)(2,1)S(1)}, bf16[8,7680]{1,0:T(8,128)(2,1)S(1)}, u32[]{:S(2)}, u32[]{:S(2)}) collective-permute-start(bf16[8,7680]{1,0:T(8,128)(2,1)S(1)} %constant_dynamic-update-slice_fusion), channel_id=1, source_target_pairs={{0,7},{1,0},{2,1},{3,2},{4,3},{5,4},{6,5},{7,6},{8,15},{9,8},{10,9... | collective-permute-start | bytes 368648 | tf_op jit(solution)/shard_map/ppermute | solution.py:138
  7.8 11.8 %collective-permute-start = (bf16[8,7680]{1,0:T(8,128)(2,1)S(1)}, bf16[8,7680]{1,0:T(8,128)(2,1)S(1)}, u32[]{:S(2)}, u32[]{:S(2)}) collective-permute-start(bf16[8,7680]{1,0:T(8,128)(2,1)S(1)} %constant_dynamic-update-slice_fusion), channel_id=1, source_target_pairs={{0,1},{1,2},{2,3},{3,4},{4,5},{5,6},{6,7},{7,0},{8,9},{9,10},{10,1... | collective-permute-start | bytes 368648 | tf_op jit(solution)/shard_map/ppermute | solution.py:133
  10.8 44.9 %copy-start.28 = (s32[128]{0:T(128)}, s32[128]{0:T(128)S(1)}, u32[]{:S(2)}) copy-start(s32[128]{0:T(128)S(1)} %broadcast_add_fusion.1) | copy-start | bytes 1540
  16.6 5.4 %collective-permute-start.3 = (bf16[8,7680]{1,0:T(8,128)(2,1)S(1)}, bf16[8,7680]{1,0:T(8,128)(2,1)S(1)}, u32[]{:S(2)}, u32[]{:S(2)}) collective-permute-start(bf16[8,7680]{1,0:T(8,128)(2,1)S(1)} %collective-permute-done.1), channel_id=1, source_target_pairs={{0,7},{1,0},{2,1},{3,2},{4,3},{5,4},{6,5},{7,6},{8,15},{9,8},{10,9... | collective-permute-start | bytes 368648 | tf_op jit(solution)/shard_map/ppermute | solution.py:138
  19.5 5.5 %collective-permute-start.2 = (bf16[8,7680]{1,0:T(8,128)(2,1)S(1)}, bf16[8,7680]{1,0:T(8,128)(2,1)S(1)}, u32[]{:S(2)}, u32[]{:S(2)}) collective-permute-start(bf16[8,7680]{1,0:T(8,128)(2,1)S(1)} %collective-permute-done), channel_id=1, source_target_pairs={{0,1},{1,2},{2,3},{3,4},{4,5},{5,6},{6,7},{7,0},{8,9},{9,10},{10,1... | collective-permute-start | bytes 368648 | tf_op jit(solution)/shard_map/ppermute | solution.py:133
  22.0 9.2 %collective-permute-start.5 = (bf16[8,7680]{1,0:T(8,128)(2,1)S(1)}, bf16[8,7680]{1,0:T(8,128)(2,1)S(1)}, u32[]{:S(2)}, u32[]{:S(2)}) collective-permute-start(bf16[8,7680]{1,0:T(8,128)(2,1)S(1)} %collective-permute-done.3), channel_id=1, source_target_pairs={{0,7},{1,0},{2,1},{3,2},{4,3},{5,4},{6,5},{7,6},{8,15},{9,8},{10,9... | collective-permute-start | bytes 368648 | tf_op jit(solution)/shard_map/ppermute | solution.py:138
  25.0 5.5 %collective-permute-start.4 = (bf16[8,7680]{1,0:T(8,128)(2,1)S(1)}, bf16[8,7680]{1,0:T(8,128)(2,1)S(1)}, u32[]{:S(2)}, u32[]{:S(2)}) collective-permute-start(bf16[8,7680]{1,0:T(8,128)(2,1)S(1)} %collective-permute-done.2), channel_id=1, source_target_pairs={{0,1},{1,2},{2,3},{3,4},{4,5},{5,6},{6,7},{7,0},{8,9},{9,10},{10,1... | collective-permute-start | bytes 368648 | tf_op jit(solution)/shard_map/ppermute | solution.py:133
  30.6 5.5 %collective-permute-start.6 = (bf16[8,7680]{1,0:T(8,128)(2,1)S(1)}, bf16[8,7680]{1,0:T(8,128)(2,1)S(1)}, u32[]{:S(2)}, u32[]{:S(2)}) collective-permute-start(bf16[8,7680]{1,0:T(8,128)(2,1)S(1)} %collective-permute-done.4), channel_id=1, source_target_pairs={{0,1},{1,2},{2,3},{3,4},{4,5},{5,6},{6,7},{7,0},{8,9},{9,10},{10,1... | collective-permute-start | bytes 368648 | tf_op jit(solution)/shard_map/ppermute | solution.py:133
  47.3 30.4 %all-to-all-start = ((bf16[16,5,7680]{2,1,0:T(8,128)(2,1)}), bf16[16,5,7680]{2,1,0:T(8,128)(2,1)}, u32[]{:S(2)}, u32[]{:S(2)}) async-start(bf16[16,5,7680]{2,1,0:T(8,128)(2,1)} %broadcast_select_fusion), calls=%async_computation | async-start | bytes 3932160 | tf_op jit(solution)/shard_map/all_to_all | solution.py:158
  55.7 36.1 %copy-start.15 = (f32[1152]{0:T(1024)}, f32[1152]{0:T(1024)S(1)}, u32[]{:S(2)}) copy-start(f32[1152]{0:T(1024)S(1)} %convert_element_type.91) | copy-start | bytes 13828
  55.7 36.1 %copy-start.21 = (f32[128]{0:T(128)}, f32[128]{0:T(128)S(1)}, u32[]{:S(2)}) copy-start(f32[128]{0:T(128)S(1)} %add_rsqrt_fusion) | copy-start | bytes 1540
  55.8 36.0 %copy-start.24 = (f32[128,5]{0,1:T(8,128)}, f32[128,5]{0,1:T(8,128)S(1)}, u32[]{:S(2)}) copy-start(f32[128,5]{0,1:T(8,128)S(1)} %fusion.34) | copy-start | bytes 7684
  56.5 39.6 %copy-start.12 = (f32[128,32]{0,1:T(8,128)}, f32[128,32]{0,1:T(8,128)S(1)}, u32[]{:S(2)}) copy-start(f32[128,32]{0,1:T(8,128)S(1)} %get-tuple-element.14) | copy-start | bytes 49156
  98.6 29.6 %copy-start.6 = (bf16[128,768]{1,0:T(8,128)(2,1)}, bf16[128,768]{1,0:T(8,128)(2,1)S(1)}, u32[]{:S(2)}) copy-start(bf16[128,768]{1,0:T(8,128)(2,1)S(1)} %pad_maximum_fusion.1) | copy-start | bytes 589828
  98.6 11.2 %collective-permute-start.7 = (bf16[128,768]{1,0:T(8,128)(2,1)S(1)}, bf16[128,768]{1,0:T(8,128)(2,1)S(1)}, u32[]{:S(2)}, u32[]{:S(2)}) collective-permute-start(bf16[128,768]{1,0:T(8,128)(2,1)S(1)} %pad_maximum_fusion.1), channel_id=1, source_target_pairs={{0,1},{1,2},{2,3},{3,4},{4,5},{5,6},{6,7},{7,8},{8,9},{9,10},{10,1... | collective-permute-start | bytes 589832 | tf_op jit(solution)/shard_map/ppermute | solution.py:22
  109.8 11.3 %collective-permute-start.8 = (bf16[128,768]{1,0:T(8,128)(2,1)S(1)}, bf16[128,768]{1,0:T(8,128)(2,1)}, u32[]{:S(2)}, u32[]{:S(2)}) collective-permute-start(bf16[128,768]{1,0:T(8,128)(2,1)S(1)} %collective-permute-done.7), channel_id=1, source_target_pairs={{0,1},{1,2},{2,3},{3,4},{4,5},{5,6},{6,7},{7,8},{8,9},{9,10},{10,1... | collective-permute-start | bytes 589832 | tf_op jit(solution)/shard_map/ppermute | solution.py:22
  121.1 23.4 %collective-permute-start.9 = (bf16[128,768]{1,0:T(8,128)(2,1)}, bf16[128,768]{1,0:T(8,128)(2,1)}, u32[]{:S(2)}, u32[]{:S(2)}) collective-permute-start(bf16[128,768]{1,0:T(8,128)(2,1)} %collective-permute-done.8), channel_id=1, source_target_pairs={{0,1},{1,2},{2,3},{3,4},{4,5},{5,6},{6,7},{7,8},{8,9},{9,10},{10,1... | collective-permute-start | bytes 589832 | tf_op jit(solution)/shard_map/ppermute | solution.py:22
  133.3 24.6 %copy-start.16 = (f32[1152]{0:T(1024)S(1)}, f32[1152]{0:T(1024)}, u32[]{:S(2)}) copy-start(f32[1152]{0:T(1024)} %copy-done.15) | copy-start | bytes 13828
  133.3 24.7 %copy-start.22 = (f32[128]{0:T(128)S(1)}, f32[128]{0:T(128)}, u32[]{:S(2)}) copy-start(f32[128]{0:T(128)} %copy-done.21) | copy-start | bytes 1540
  144.5 11.4 %collective-permute-start.10 = (bf16[128,768]{1,0:T(8,128)(2,1)}, bf16[128,768]{1,0:T(8,128)(2,1)S(1)}, u32[]{:S(2)}, u32[]{:S(2)}) collective-permute-start(bf16[128,768]{1,0:T(8,128)(2,1)} %collective-permute-done.9), channel_id=1, source_target_pairs={{0,1},{1,2},{2,3},{3,4},{4,5},{5,6},{6,7},{7,8},{8,9},{9,10},{10,1... | collective-permute-start | bytes 589832 | tf_op jit(solution)/shard_map/ppermute | solution.py:22
  147.5 21.9 %copy-start.13 = (f32[128,32]{0,1:T(8,128)S(1)}, f32[128,32]{0,1:T(8,128)}, u32[]{:S(2)}) copy-start(f32[128,32]{0,1:T(8,128)} %copy-done.12) | copy-start | bytes 49156
  147.5 21.9 %copy-start.14 = (f32[128,32]{0,1:T(8,128)S(1)}, f32[128,32]{0,1:T(8,128)}, u32[]{:S(2)}) copy-start(f32[128,32]{0,1:T(8,128)} %get-tuple-element.15) | copy-start | bytes 49156
  156.0 11.3 %collective-permute-start.11 = (bf16[128,768]{1,0:T(8,128)(2,1)S(1)}, bf16[128,768]{1,0:T(8,128)(2,1)}, u32[]{:S(2)}, u32[]{:S(2)}) collective-permute-start(bf16[128,768]{1,0:T(8,128)(2,1)S(1)} %collective-permute-done.10), channel_id=1, source_target_pairs={{0,1},{1,2},{2,3},{3,4},{4,5},{5,6},{6,7},{7,8},{8,9},{9,10},{10,1... | collective-permute-start | bytes 589832 | tf_op jit(solution)/shard_map/ppermute | solution.py:22
  167.3 35.9 %copy-start.10 = (bf16[128,768]{1,0:T(8,128)(2,1)S(1)}, bf16[128,768]{1,0:T(8,128)(2,1)}, u32[]{:S(2)}) copy-start(bf16[128,768]{1,0:T(8,128)(2,1)} %copy-done.9) | copy-start | bytes 589828
  167.3 11.5 %collective-permute-start.12 = (bf16[128,768]{1,0:T(8,128)(2,1)}, bf16[128,768]{1,0:T(8,128)(2,1)S(1)}, u32[]{:S(2)}, u32[]{:S(2)}) collective-permute-start(bf16[128,768]{1,0:T(8,128)(2,1)} %collective-permute-done.11), channel_id=1, source_target_pairs={{0,1},{1,2},{2,3},{3,4},{4,5},{5,6},{6,7},{7,8},{8,9},{9,10},{10,1... | collective-permute-start | bytes 589832 | tf_op jit(solution)/shard_map/ppermute | solution.py:22
  178.8 11.2 %collective-permute-start.13 = (bf16[128,768]{1,0:T(8,128)(2,1)S(1)}, bf16[128,768]{1,0:T(8,128)(2,1)S(1)}, u32[]{:S(2)}, u32[]{:S(2)}) collective-permute-start(bf16[128,768]{1,0:T(8,128)(2,1)S(1)} %collective-permute-done.12), channel_id=1, source_target_pairs={{0,1},{1,2},{2,3},{3,4},{4,5},{5,6},{6,7},{7,8},{8,9},{9,10},{10,1... | collective-permute-start | bytes 589832 | tf_op jit(solution)/shard_map/ppermute | solution.py:22
  190.0 11.2 %collective-permute-start.14 = (bf16[128,768]{1,0:T(8,128)(2,1)S(1)}, bf16[128,768]{1,0:T(8,128)(2,1)S(1)}, u32[]{:S(2)}, u32[]{:S(2)}) collective-permute-start(bf16[128,768]{1,0:T(8,128)(2,1)S(1)} %collective-permute-done.13), channel_id=1, source_target_pairs={{0,1},{1,2},{2,3},{3,4},{4,5},{5,6},{6,7},{7,8},{8,9},{9,10},{10,1... | collective-permute-start | bytes 589832 | tf_op jit(solution)/shard_map/ppermute | solution.py:22
  201.2 11.2 %collective-permute-start.15 = (bf16[128,768]{1,0:T(8,128)(2,1)S(1)}, bf16[128,768]{1,0:T(8,128)(2,1)S(1)}, u32[]{:S(2)}, u32[]{:S(2)}) collective-permute-start(bf16[128,768]{1,0:T(8,128)(2,1)S(1)} %collective-permute-done.14), channel_id=1, source_target_pairs={{0,1},{1,2},{2,3},{3,4},{4,5},{5,6},{6,7},{7,8},{8,9},{9,10},{10,1... | collective-permute-start | bytes 589832 | tf_op jit(solution)/shard_map/ppermute | solution.py:22
  212.4 11.2 %collective-permute-start.16 = (bf16[128,768]{1,0:T(8,128)(2,1)S(1)}, bf16[128,768]{1,0:T(8,128)(2,1)S(1)}, u32[]{:S(2)}, u32[]{:S(2)}) collective-permute-start(bf16[128,768]{1,0:T(8,128)(2,1)S(1)} %collective-permute-done.15), channel_id=1, source_target_pairs={{0,1},{1,2},{2,3},{3,4},{4,5},{5,6},{6,7},{7,8},{8,9},{9,10},{10,1... | collective-permute-start | bytes 589832 | tf_op jit(solution)/shard_map/ppermute | solution.py:22
  223.6 11.2 %collective-permute-start.17 = (bf16[128,768]{1,0:T(8,128)(2,1)S(1)}, bf16[128,768]{1,0:T(8,128)(2,1)S(1)}, u32[]{:S(2)}, u32[]{:S(2)}) collective-permute-start(bf16[128,768]{1,0:T(8,128)(2,1)S(1)} %collective-permute-done.16), channel_id=1, source_target_pairs={{0,1},{1,2},{2,3},{3,4},{4,5},{5,6},{6,7},{7,8},{8,9},{9,10},{10,1... | collective-permute-start | bytes 589832 | tf_op jit(solution)/shard_map/ppermute | solution.py:22
  234.8 11.2 %collective-permute-start.18 = (bf16[128,768]{1,0:T(8,128)(2,1)S(1)}, bf16[128,768]{1,0:T(8,128)(2,1)S(1)}, u32[]{:S(2)}, u32[]{:S(2)}) collective-permute-start(bf16[128,768]{1,0:T(8,128)(2,1)S(1)} %collective-permute-done.17), channel_id=1, source_target_pairs={{0,1},{1,2},{2,3},{3,4},{4,5},{5,6},{6,7},{7,8},{8,9},{9,10},{10,1... | collective-permute-start | bytes 589832 | tf_op jit(solution)/shard_map/ppermute | solution.py:22
  (18 other events, 154.6 us)
